TPU v7x, 128 devices: a whole 4x4x4 slice. The times are simulated.
128 devices in a mesh: req: 8 (over z, core), exp: 16 (over x, y).
Axes of the slice: x: 4, y: 4, z: 4, core: 2. Of those that a mesh axis runs over, the one named last changes fastest.
Arguments:
- tokens: bfloat16 [32768, 1536], P(('req', 'exp')), may hold values from -6 to 6
- attn_gain: float32 [1536], replicated, may hold values from 0.1 to 1.9
- w_query: bfloat16 [1536, 1536], P('req'), may hold values from -0.15625 to 0.15625
- key_projection: bfloat16 [1536, 256], P('req'), may hold values from -0.15625 to 0.15625
- value_projection: bfloat16 [1536, 256], P('req'), may hold values from -0.15625 to 0.15625
- w_out: bfloat16 [1536, 1536], P(None, 'req'), may hold values from -0.15625 to 0.15625
- moe_gain: float32 [1536], replicated, may hold values from 0.1 to 1.9
- w_gate: bfloat16 [32, 1536, 768], P('exp'), may hold values from -0.15625 to 0.15625
- w_up: bfloat16 [32, 1536, 768], P('exp'), may hold values from -0.15625 to 0.15625
- w_down: bfloat16 [32, 768, 1536], P('exp'), may hold values from -0.21875 to 0.21875
- routes: int32 [32768, 4], P(('req', 'exp')), may hold values from 0 to 31, all different within a row; in each aligned block of 128 rows (0 to 127, 128 to 255, ...) at most 24 rows name the same one
- gate_weights: float32 [32768, 4], P(('req', 'exp')), may hold values from 0.1 to 1
- kv_cache: bfloat16 [512, 1024, 512], P(('req', 'exp')), may hold values from -360 to 360, as said below
- lengths: int32 [512], P(('req', 'exp')), may hold values from 128 to 1024, as said below
- parents: int32 [512, 64], P(('req', 'exp')), may hold values from 0 to 62, as said below
- accepted: int32 [512], P(('req', 'exp')), may hold values from 0 to 63
Outputs:
- layer_out: bfloat16 [32768, 1536], P(('req', 'exp'))
- new_entries: bfloat16 [512, 64, 512], P(('req', 'exp'))
Inputs may be any that keep to these rules, and one draw needn't show every extreme that they name: `routes`: each row names 4 different experts; among the rows of one aligned block of 128 rows no expert is named more than 24 times, and in some block one expert exactly 24 times. `kv_cache`: cache entries are finite; slots at or after a request's length hold arbitrary values. `lengths`: some request has exactly 1024 live slots. parents[r, 0] = 0 marks the root; for i >= 1, parents[r, i] < i.
All inputs are finite; a program needn't handle non-finite values.
Results may differ from a plain program's by a relative error of at most 0.013.
The roundings to bfloat16 on the way count: a program that leaves them out, or rounds other values in their place, can miss the bound.
Values may be sent and summed in bfloat16 or wider, within the bound.
No kernel may reach another device: no remote copies, remote signals or barrier semaphores. Data moves between devices by JAX's collectives and lax.ppermute only.
A program may use at most 128 MiB of HBM per device.

v0:
```python
import math
import jax
import jax.numpy as jnp
from jax import lax
from jax.sharding import PartitionSpec as P

QUERY_HEADS = 12
KEY_VALUE_HEADS = 2
HEAD_SIZE = 128
EXPERTS = 32
TOP = 4
DRAFT_TOKENS = 64
CAP = 24
BLOCK_ROWS = 128
eps_norm = 1e-06
rope_base = 1000000.0


def rms_scale(token_rows, gain_vec):
    widened = token_rows.astype(jnp.float32)
    inverse = lax.rsqrt(jnp.mean(widened * widened, axis=-1, keepdims=True) + eps_norm)
    return (widened * inverse * gain_vec).astype(jnp.bfloat16)


def rotate(values, positions):
    row_count = values.shape[0]
    head_count = values.shape[1] // HEAD_SIZE
    half_size = HEAD_SIZE // 2
    reshaped_rows = values.reshape(row_count, head_count, HEAD_SIZE)
    frequency = rope_base ** (-jnp.arange(half_size, dtype=jnp.float32) / half_size)
    angles = positions.astype(jnp.float32)[:, None] * frequency[None, :]
    cosine = jnp.cos(angles)[:, None, :]
    sine_part = jnp.sin(angles)[:, None, :]
    leading = reshaped_rows[..., :half_size]
    second = reshaped_rows[..., half_size:]
    turned = jnp.concatenate(
        [leading * cosine - second * sine_part, second * cosine + leading * sine_part], axis=-1
    )
    return turned.reshape(row_count, head_count * HEAD_SIZE)


def ancestry(parents):
    node_count = parents.shape[-1]
    node_index = jnp.arange(node_count, dtype=jnp.int32)
    parent_step = (parents[..., :, None] == node_index[None, None, :]).astype(jnp.float32)
    closure = jnp.maximum(parent_step, jnp.eye(node_count, dtype=jnp.float32)[None])
    for squaring in range(max(1, (node_count - 1).bit_length())):
        closure = jnp.minimum(jnp.einsum("rij,rjk->rik", closure, closure), 1.0)
    tree_depth = jnp.sum(closure, axis=-1).astype(jnp.int32) - 1
    return (closure, tree_depth)


def attend(query_rows, tree_key_value, cached_row_block, length, closure):
    tree_drafts = query_rows.shape[0]
    queries_per_group = QUERY_HEADS // KEY_VALUE_HEADS
    key_value_width = KEY_VALUE_HEADS * HEAD_SIZE
    reshaped_rows = query_rows.reshape(tree_drafts, KEY_VALUE_HEADS, queries_per_group, HEAD_SIZE)
    cached_key_rows = cached_row_block[:, :key_value_width].reshape(-1, KEY_VALUE_HEADS, HEAD_SIZE)
    cached_value_rows = cached_row_block[:, key_value_width:].reshape(
        -1, KEY_VALUE_HEADS, HEAD_SIZE
    )
    tree_key_rows = tree_key_value[:, :key_value_width].reshape(-1, KEY_VALUE_HEADS, HEAD_SIZE)
    tree_value_rows = tree_key_value[:, key_value_width:].reshape(-1, KEY_VALUE_HEADS, HEAD_SIZE)
    scale = 1.0 / math.sqrt(HEAD_SIZE)
    cache_scores = (
        jnp.einsum(
            "igsd,jgd->gsij", reshaped_rows, cached_key_rows, preferred_element_type=jnp.float32
        )
        * scale
    )
    draft_scores = (
        jnp.einsum(
            "igsd,jgd->gsij", reshaped_rows, tree_key_rows, preferred_element_type=jnp.float32
        )
        * scale
    )
    live_cache = (jnp.arange(cached_row_block.shape[0]) < length)[None, None, None, :]
    live_draft = (closure > 0.5)[None, None, :, :]
    cache_scores = jnp.where(live_cache, cache_scores, -1e30)
    draft_scores = jnp.where(live_draft, draft_scores, -1e30)
    highest = jnp.maximum(jnp.max(cache_scores, axis=-1), jnp.max(draft_scores, axis=-1))[..., None]
    cache_weight = jnp.exp(cache_scores - highest)
    draft_weight = jnp.exp(draft_scores - highest)
    running = jnp.sum(cache_weight, axis=-1, keepdims=True) + jnp.sum(
        draft_weight, axis=-1, keepdims=True
    )
    cache_probs = (cache_weight / running).astype(jnp.bfloat16)
    draft_probs = (draft_weight / running).astype(jnp.bfloat16)
    context = jnp.einsum(
        "gsij,jgd->igsd", cache_probs, cached_value_rows, preferred_element_type=jnp.float32
    )
    context = context + jnp.einsum(
        "gsij,jgd->igsd", draft_probs, tree_value_rows, preferred_element_type=jnp.float32
    )
    return context.reshape(tree_drafts, QUERY_HEADS * HEAD_SIZE).astype(jnp.bfloat16)


def compact(kv_rows, closure, tree_depth, accepted):
    path_mask = jnp.take_along_axis(closure, accepted[:, None, None], axis=1)[:, 0, :]
    level = jnp.arange(kv_rows.shape[1], dtype=jnp.int32)
    select = (
        path_mask[:, None, :] * (tree_depth[:, None, :] == level[None, :, None]).astype(jnp.float32)
    ).astype(jnp.bfloat16)
    return jnp.einsum("rtj,rjw->rtw", select, kv_rows, preferred_element_type=jnp.float32).astype(
        jnp.bfloat16
    )


def slot_tables(routes, gate_weights, capacity):
    rows = routes.shape[0]
    expert_ids = jnp.arange(EXPERTS, dtype=jnp.int32)
    picks = routes[:, :, None] == expert_ids[None, None, :]
    chosen = jnp.sum(picks.astype(jnp.int32), axis=1).astype(jnp.bfloat16)
    row_ids = jnp.arange(rows, dtype=jnp.int32)
    same_block = row_ids[None, :] // BLOCK_ROWS == row_ids[:, None] // BLOCK_ROWS
    before = ((row_ids[None, :] < row_ids[:, None]) & same_block).astype(jnp.bfloat16)
    earlier = jnp.dot(before, chosen, preferred_element_type=jnp.float32).astype(jnp.int32)
    slot_number = jnp.sum(jnp.where(picks, earlier[:, None, :], 0), axis=2)
    slot_index = routes * capacity + slot_number
    slot_ids = jnp.arange(EXPERTS * capacity, dtype=jnp.int32)
    hit = slot_index[:, :, None] == slot_ids[None, None, :]
    place = jnp.sum(hit.astype(jnp.bfloat16), axis=1)
    weight = jnp.sum(jnp.where(hit, gate_weights[:, :, None], 0.0), axis=1)
    weight_hi = weight.astype(jnp.bfloat16)
    weight_lo = (weight - weight_hi.astype(jnp.float32)).astype(jnp.bfloat16)
    return (place, weight_hi, weight_lo)


def pack_slots(token_rows, place):
    return jnp.einsum("ts,td->sd", place, token_rows, preferred_element_type=jnp.bfloat16)


def expert_products(received, w_gate, w_up, w_down):
    gate_part = jnp.einsum("pekd,edf->pekf", received, w_gate, preferred_element_type=jnp.float32)
    up_part = jnp.einsum("pekd,edf->pekf", received, w_up, preferred_element_type=jnp.float32)
    hidden = (jnp.maximum(gate_part, 0.0) * up_part).astype(jnp.bfloat16)
    return jnp.einsum("pekf,efd->pekd", hidden, w_down, preferred_element_type=jnp.float32).astype(
        jnp.bfloat16
    )


def combine_picks(returned_rows, weight_hi, weight_lo):
    layer_width = returned_rows.shape[-1]
    rows = weight_hi.shape[0]
    flat_rows = returned_rows.reshape(-1, layer_width)
    both = jnp.concatenate([weight_hi, weight_lo], axis=0)
    mixed = jnp.dot(both, flat_rows, preferred_element_type=jnp.float32)
    return mixed[:rows] + mixed[rows:]


def routed_whole(moe_in, place, weight_hi, weight_lo, w_gate, w_up, w_down):
    capacity = place.shape[1] // EXPERTS
    buffer = pack_slots(moe_in, place)
    peer_count = lax.axis_size("exp")
    reshaped_rows = buffer.reshape(peer_count, w_gate.shape[0], capacity, moe_in.shape[1])
    produced = expert_products(
        lax.all_to_all(reshaped_rows, "exp", split_axis=0, concat_axis=0, tiled=True),
        w_gate,
        w_up,
        w_down,
    )
    returned_rows = lax.all_to_all(produced, "exp", split_axis=0, concat_axis=0, tiled=True)
    return combine_picks(returned_rows, weight_hi, weight_lo)


def local(
    tokens,
    attn_gain,
    w_query,
    key_projection,
    value_projection,
    w_out,
    moe_gain,
    w_gate,
    w_up,
    w_down,
    routes,
    gate_weights,
    kv_cache,
    lengths,
    parents,
    accepted,
):
    rows_here = tokens.shape[0]
    local_reqs = kv_cache.shape[0]
    normed = rms_scale(tokens, attn_gain)
    closure, tree_depth = ancestry(parents)
    positions = (lengths[:, None] + tree_depth).reshape(-1)
    query_sum = jnp.dot(
        normed,
        lax.all_gather(w_query, "req", axis=0, tiled=True),
        preferred_element_type=jnp.float32,
    )
    key_sum = jnp.dot(
        normed,
        lax.all_gather(key_projection, "req", axis=0, tiled=True),
        preferred_element_type=jnp.float32,
    )
    value_sum = jnp.dot(
        normed,
        lax.all_gather(value_projection, "req", axis=0, tiled=True),
        preferred_element_type=jnp.float32,
    )
    query_rows = rotate(query_sum, positions).astype(jnp.bfloat16)
    tree_key_value = jnp.concatenate([rotate(key_sum, positions), value_sum], axis=1).astype(
        jnp.bfloat16
    )
    query_req = query_rows.reshape(local_reqs, DRAFT_TOKENS, query_rows.shape[1])
    key_value_request = tree_key_value.reshape(local_reqs, DRAFT_TOKENS, tree_key_value.shape[1])
    w_out_full = lax.all_gather(w_out, "req", axis=1, tiled=True)
    chunk_count = rows_here // BLOCK_ROWS
    context_all = jax.vmap(attend)(
        query_req, key_value_request, kv_cache, lengths, closure
    ).reshape(rows_here, -1)
    place, weight_hi, weight_lo = slot_tables(routes, gate_weights, CAP)
    outs = []
    for chunk in range(chunk_count):
        rw = slice(chunk * BLOCK_ROWS, (chunk + 1) * BLOCK_ROWS)
        attn_out = jnp.dot(context_all[rw], w_out_full, preferred_element_type=jnp.float32)
        residual = (tokens[rw].astype(jnp.float32) + attn_out).astype(jnp.bfloat16)
        moe_in = rms_scale(residual, moe_gain)
        mixed = routed_whole(moe_in, place[rw], weight_hi[rw], weight_lo[rw], w_gate, w_up, w_down)
        outs.append((residual.astype(jnp.float32) + mixed).astype(jnp.bfloat16))
    layer_out = jnp.concatenate(outs, axis=0)
    new_entries = compact(key_value_request, closure, tree_depth, accepted)
    return (layer_out, new_entries)


def solution(mesh):
    return jax.shard_map(
        local,
        mesh=mesh,
        in_specs=(
            P(("req", "exp"), None),
            P(),
            P("req", None),
            P("req", None),
            P("req", None),
            P(None, "req"),
            P(),
            P("exp", None, None),
            P("exp", None, None),
            P("exp", None, None),
            P(("req", "exp"), None),
            P(("req", "exp"), None),
            P(("req", "exp"), None, None),
            P(("req", "exp")),
            P(("req", "exp"), None),
            P(("req", "exp")),
        ),
        out_specs=(P(("req", "exp"), None), P(("req", "exp"), None, None)),
        check_vma=False,
    )
```

profile of v0, /device:TPU:0, one launch (start us, length us, event | category | flops | bytes accessed | tf_op | source)
XLA Modules:
  0.0 250.2 jit_solution(5174756153162118243)
XLA Ops:
  7.2 0.7 all-gather.3.cloned.1.call-update
  8.0 0.7 all-gather.5.cloned.1.call-update
  8.7 1.3 convolution_minimum_fusion.4
  10.0 0.3 convolution_minimum_fusion.2
  10.3 0.3 broadcast_compare_fusion
  10.7 0.7 convert_add_fusion
  11.6 0.3 multiply_cosine_fusion
  12.0 0.8 copy.126
  12.8 0.2 fusion.36
  13.0 15.6 %all_gather.13 = bf16[1536,256]{1,0:T(8,128)(2,1)S(1)} all-gather(bf16[192,256]{1,0:T(8,128)(2,1)S(1)} %copy-done.16), channel_id=1, replica_groups=mesh['req'=8,'exp'=16] {'req'}, dimensions={0}, use_global_device_ids=true | all-gather | bytes 884736 | tf_op jit(solution)/shard_map/all_gather | solution.py:196
  28.6 0.6 fusion.133
  29.5 0.7 copy.122
  30.2 4.6 %fusion.137 = (bf16[4,1024,256]{2,1,0:T(8,128)(2,1)}, bf16[4,1024,256]{2,1,0:T(8,128)(2,1)}) fusion(bf16[4,1024,512]{2,1,0:T(8,128)(2,1)} %param.28), kind=kLoop, calls=%fused_computation.165 | loop fusion | bytes 8388608 | tf_op jit(solution)/shard_map/vmap()/slice | solution.py:59
  34.8 3.0 %copy.161 = bf16[4,1024,256]{1,2,0:T(8,128)(2,1)S(1)} copy(bf16[4,1024,256]{2,1,0:T(8,128)(2,1)} %get-tuple-element.5) | data formatting | bytes 4194304
  37.8 15.3 %all_gather.14 = bf16[1536,256]{1,0:T(8,128)(2,1)S(1)} all-gather(bf16[192,256]{1,0:T(8,128)(2,1)} %param.20), channel_id=1, replica_groups=mesh['req'=8,'exp'=16] {'req'}, dimensions={0}, use_global_device_ids=true | all-gather | bytes 884736 | tf_op jit(solution)/shard_map/all_gather | solution.py:201
  53.1 1.8 convolution_convert_fusion.1
  54.9 1.6 reshape.304
  56.5 4.0 %copy.164 = bf16[4,1024,256]{1,2,0:T(8,128)(2,1)} copy(bf16[4,1024,256]{2,1,0:T(8,128)(2,1)} %get-tuple-element.4) | data formatting | bytes 4194304
  60.6 1.0 subtract_convert_fusion.2
  61.7 0.2 convolution_convert_fusion.2
  62.0 0.4 fusion.39
  62.6 4.4 %fusion.135 = f32[256,1536]{0,1:T(8,128)S(1)} fusion(bf16[1536,1536]{1,0:T(8,128)(2,1)} %all-gather.3.cloned.1.call-done, bf16[256,1536]{1,0:T(8,128)(2,1)S(1)} %copy-done.2, f32[1536]{0:T(1024)} %param.17, f32[256]{0:T(256)} %copy-done.21), kind=kOutput, calls=%fused_computation.164 | convolution fusion | flops 1209532416 | bytes 7085056 | tf_op jit(solution)/shard_map/dot_general | solution.py:189
  67.0 0.2 subtract_convert_fusion.1
  67.3 0.9 pad_maximum_fusion
  68.2 1.5 copy.118
  69.7 0.9 fusion.142
  70.6 2.1 bitcast_reduce_fusion
  72.7 0.4 fusion.59
  73.1 3.1 %fusion.1 = f32[4,2,6,64]{3,2,1,0:T(8,128)S(1)} fusion(f32[4,2,64,6,1024]{4,2,3,1,0:T(8,128)S(1)} %get-tuple-element.25, f32[4,2,6,64]{3,2,1,0:T(8,128)S(1)} %max.25, pred[4,1024]{1,0:T(4,128)(4,1)S(1)} %iota_compare_fusion.8), kind=kLoop, calls=%fused_computation.6 | loop fusion | flops 12579840 | bytes 12611584 | tf_op jit(solution)/shard_map/vmap()/reduce_sum | solution.py:84
  76.3 0.5 fusion.74
  76.8 1.1 copy-done.5
  77.8 3.9 %fusion.40 = bf16[4,64,2,6,128]{4,1,3,2,0:T(8,128)(2,1)S(1)} fusion(f32[4,2,128,6,64]{2,4,3,1,0:T(8,128)S(1)} %fusion.74, bf16[4,1024,2,128,1]{1,3,4,2,0:T(8,128)(2,1)S(1)} %bitcast.120, f32[4,2,64,6,1024]{4,2,3,1,0:T(8,128)S(1)} %get-tuple-element.25, f32[4,2,6,64]{3,2,1,0:T(8,128)S(1)} %add.113, f32[4,2,6,64]{3,2,1,0:T(8,128)S(1)} %max.25, ...), kind=kOutput, calls=%fused_computation.46 | convolution fusion | flops 821821440 | bytes 17068032 | tf_op jit(solution)/shard_map/vmap(gsij,jgd->igsd)/dot_general | solution.py:89
  81.9 0.3 copy.133
  82.2 0.4 slice.78
  82.6 1.7 all-gather.5.cloned.1.call-done
  84.3 4.1 %multiply_reduce_fusion.1 = (f32[128]{0:T(128)S(1)}, f32[128,1536]{1,0:T(8,128)S(1)}) fusion(bf16[128,1536]{1,0:T(8,128)(2,1)S(1)} %slice.78, bf16[1536,1536]{0,1:T(8,128)(2,1)} %all-gather.5.cloned.1.call-done, bf16[256,1536]{1,0:T(8,128)(2,1)S(1)} %copy-done.3), kind=kOutput, calls=%fused_computation.75 | convolution fusion | flops 605159296 | bytes 6291968 | tf_op jit(solution)/shard_map/dot_general | solution.py:219
  88.4 2.3 fusion.78
  90.7 6.9 %all-to-all-start = ((bf16[16,2,24,1536]{3,2,1,0:T(8,128)(2,1)}), bf16[16,2,24,1536]{3,2,1,0:T(8,128)(2,1)}, u32[]{:S(2)}, u32[]{:S(2)}) async-start(bf16[16,2,24,1536]{3,2,1,0:T(8,128)(2,1)} %bitcast.14), calls=%async_computation | async-start | bytes 4718592 | tf_op jit(solution)/shard_map/all_to_all | solution.py:157
  97.6 0.3 copy.137
  97.8 0.4 slice.86
  98.3 4.1 %multiply_reduce_fusion = (f32[128]{0:T(128)S(1)}, f32[128,1536]{1,0:T(8,128)S(1)}) fusion(bf16[128,1536]{1,0:T(8,128)(2,1)S(1)} %slice.86, bf16[1536,1536]{0,1:T(8,128)(2,1)} %all-gather.5.cloned.1.call-done, bf16[256,1536]{1,0:T(8,128)(2,1)S(1)} %copy-done.3), kind=kOutput, calls=%fused_computation.73 | convolution fusion | flops 605159296 | bytes 6291968 | tf_op jit(solution)/shard_map/dot_general | solution.py:219
  102.4 0.9 copy-done
  103.2 2.3 fusion.79
  105.5 25.7 %all-to-all-done = bf16[16,2,24,1536]{3,2,1,0:T(8,128)(2,1)} async-done(((bf16[16,2,24,1536]{3,2,1,0:T(8,128)(2,1)}), bf16[16,2,24,1536]{3,2,1,0:T(8,128)(2,1)}, u32[]{:S(2)}, u32[]{:S(2)}) %all-to-all-start) | async-done | bytes 2359328 | tf_op jit(solution)/shard_map/all_to_all | solution.py:157
  131.2 5.3 %all-to-all-start.2 = ((bf16[16,2,24,1536]{3,2,1,0:T(8,128)(2,1)}), bf16[16,2,24,1536]{3,2,1,0:T(8,128)(2,1)S(1)}, u32[]{:S(2)}, u32[]{:S(2)}) async-start(bf16[16,2,24,1536]{3,2,1,0:T(8,128)(2,1)} %bitcast.24), calls=%async_computation.2 | async-start | bytes 4718592 | tf_op jit(solution)/shard_map/all_to_all | solution.py:157
  136.6 6.5 %fusion.9 = f32[2,16,24,768]{3,2,1,0:T(8,128)} fusion(bf16[2,1536,768]{2,1,0:T(8,128)(2,1)} %param.24, bf16[16,2,24,1536]{3,2,1,0:T(8,128)(2,1)} %all-to-all-done), kind=kOutput, calls=%fused_computation.14 | convolution fusion | flops 1811939328 | bytes 9437184 | tf_op jit(solution)/shard_map/pekd,edf->pekf/dot_general | solution.py:135
  143.1 10.4 %fusion.25 = bf16[16,2,24,1536]{3,2,0,1:T(8,128)(2,1)} fusion(bf16[2,768,1536]{2,1,0:T(8,128)(2,1)} %param.25, f32[2,16,24,768]{3,2,1,0:T(8,128)} %fusion.9, bf16[2,1536,768]{2,1,0:T(8,128)(2,1)} %param.23, bf16[16,2,24,1536]{3,2,1,0:T(8,128)(2,1)} %all-to-all-done), kind=kOutput, calls=%fused_computation.26 | convolution fusion | flops 3626827776 | bytes 16515072 | tf_op jit(solution)/shard_map/pekf,efd->pekd/dot_general | solution.py:137
  153.5 3.4 %copy.136 = bf16[16,2,24,1536]{3,2,1,0:T(8,128)(2,1)} copy(bf16[16,2,24,1536]{3,2,0,1:T(8,128)(2,1)} %fusion.25) | data formatting | bytes 4718592 | tf_op jit(solution)/shard_map/convert_element_type | solution.py:137
  156.9 12.0 %all-to-all-done.2 = bf16[16,2,24,1536]{3,2,1,0:T(8,128)(2,1)S(1)} async-done(((bf16[16,2,24,1536]{3,2,1,0:T(8,128)(2,1)}), bf16[16,2,24,1536]{3,2,1,0:T(8,128)(2,1)S(1)}, u32[]{:S(2)}, u32[]{:S(2)}) %all-to-all-start.2) | async-done | bytes 2359328 | tf_op jit(solution)/shard_map/all_to_all | solution.py:157
  168.9 1.4 copy-done.4
  170.3 4.0 %all-to-all-start.1 = ((bf16[16,2,24,1536]{3,2,1,0:T(8,128)(2,1)}), bf16[16,2,24,1536]{3,2,1,0:T(8,128)(2,1)S(1)}, u32[]{:S(2)}, u32[]{:S(2)}) async-start(bf16[16,2,24,1536]{3,2,1,0:T(8,128)(2,1)} %copy.136), calls=%async_computation.1 | async-start | bytes 4718592 | tf_op jit(solution)/shard_map/all_to_all | solution.py:162
  174.3 0.1 copy.141
  174.6 1.5 gather_fusion
  176.1 6.5 %fusion.7 = f32[2,16,24,768]{3,2,1,0:T(8,128)} fusion(bf16[2,1536,768]{2,1,0:T(8,128)(2,1)} %param.24, bf16[16,2,24,1536]{3,2,1,0:T(8,128)(2,1)} %copy-done.4), kind=kOutput, calls=%fused_computation.12 | convolution fusion | flops 1811939328 | bytes 9437184 | tf_op jit(solution)/shard_map/pekd,edf->pekf/dot_general | solution.py:135
  182.6 10.4 %fusion.22 = bf16[16,2,24,1536]{3,2,0,1:T(8,128)(2,1)} fusion(bf16[2,768,1536]{2,1,0:T(8,128)(2,1)} %param.25, f32[2,16,24,768]{3,2,1,0:T(8,128)} %fusion.7, bf16[2,1536,768]{2,1,0:T(8,128)(2,1)} %param.23, bf16[16,2,24,1536]{3,2,1,0:T(8,128)(2,1)} %copy-done.4), kind=kOutput, calls=%fused_computation.25 | convolution fusion | flops 3626827776 | bytes 16515072 | tf_op jit(solution)/shard_map/pekf,efd->pekd/dot_general | solution.py:137
  193.0 3.4 %copy.140 = bf16[16,2,24,1536]{3,2,1,0:T(8,128)(2,1)} copy(bf16[16,2,24,1536]{3,2,0,1:T(8,128)(2,1)} %fusion.22) | data formatting | bytes 4718592 | tf_op jit(solution)/shard_map/convert_element_type | solution.py:137
  196.4 8.2 %all-to-all-done.1 = bf16[16,2,24,1536]{3,2,1,0:T(8,128)(2,1)S(1)} async-done(((bf16[16,2,24,1536]{3,2,1,0:T(8,128)(2,1)}), bf16[16,2,24,1536]{3,2,1,0:T(8,128)(2,1)S(1)}, u32[]{:S(2)}, u32[]{:S(2)}) %all-to-all-start.1) | async-done | bytes 2359328 | tf_op jit(solution)/shard_map/all_to_all | solution.py:162
  204.6 4.7 %all-to-all-start.3 = ((bf16[16,2,24,1536]{3,2,1,0:T(8,128)(2,1)}), bf16[16,2,24,1536]{3,2,1,0:T(8,128)(2,1)}, u32[]{:S(2)}, u32[]{:S(2)}) async-start(bf16[16,2,24,1536]{3,2,1,0:T(8,128)(2,1)} %copy.140), calls=%async_computation.3 | async-start | bytes 4718592 | tf_op jit(solution)/shard_map/all_to_all | solution.py:162
  209.3 0.4 select_reduce_fusion
  209.7 0.9 convolution_convert_fusion
  210.8 0.8 fusion.80
  211.7 28.1 %all-to-all-done.3 = bf16[16,2,24,1536]{3,2,1,0:T(8,128)(2,1)} async-done(((bf16[16,2,24,1536]{3,2,1,0:T(8,128)(2,1)}), bf16[16,2,24,1536]{3,2,1,0:T(8,128)(2,1)}, u32[]{:S(2)}, u32[]{:S(2)}) %all-to-all-start.3) | async-done | bytes 2359328 | tf_op jit(solution)/shard_map/all_to_all | solution.py:162
  239.8 2.4 fusion.84
  242.4 0.9 pad_maximum_fusion.1
  (79 shorter events, 1.7 us)
Async XLA Ops:
  7.2 5.6 %copy-start.2 = (bf16[256,1536]{1,0:T(8,128)(2,1)S(1)}, bf16[256,1536]{1,0:T(8,128)(2,1)}, u32[]{:S(2)}) copy-start(bf16[256,1536]{1,0:T(8,128)(2,1)} %param.16) | copy-start | bytes 2359300
  7.2 5.8 %copy-start.16 = (bf16[192,256]{1,0:T(8,128)(2,1)S(1)}, bf16[192,256]{1,0:T(8,128)(2,1)}, u32[]{:S(2)}) copy-start(bf16[192,256]{1,0:T(8,128)(2,1)} %param.19) | copy-start | bytes 294916
  7.2 21.4 %copy-start.22 = (f32[1536]{0:T(1024)S(1)}, f32[1536]{0:T(1024)}, u32[]{:S(2)}) copy-start(f32[1536]{0:T(1024)} %param.17) | copy-start | bytes 18436
  7.2 55.4 %all-gather.3.cloned.1.call-start = ((), (), s32[]{:S(2)}) async-start(), calls=%async_computation.4 | async-start | bytes 5308416 | tf_op jit(solution)/shard_map/all_gather | solution.py:191
  7.9 76.4 %all-gather.5.cloned.1.call-start = ((), (), s32[]{:S(2)}) async-start(), calls=%async_computation.5 | async-start | bytes 5308416 | tf_op jit(solution)/shard_map/all_gather | solution.py:210
  10.6 0.9 copy-start.12
  11.9 17.3 %copy-start.8 = (f32[256,64]{0,1:T(8,128)}, f32[256,64]{0,1:T(8,128)S(1)}, u32[]{:S(2)}) copy-start(f32[256,64]{0,1:T(8,128)S(1)} %get-tuple-element.20) | copy-start | bytes 196612
  11.9 17.3 %copy-start.10 = (f32[256,64]{0,1:T(8,128)}, f32[256,64]{0,1:T(8,128)S(1)}, u32[]{:S(2)}) copy-start(f32[256,64]{0,1:T(8,128)S(1)} %get-tuple-element.21) | copy-start | bytes 196612
  13.0 40.1 %copy-start.21 = (f32[256]{0:T(256)}, f32[256]{0:T(256)S(1)}, u32[]{:S(2)}) copy-start(f32[256]{0:T(256)S(1)} %add_rsqrt_fusion) | copy-start | bytes 3076
  54.9 5.7 %copy-start.17 = (s32[256,4]{0,1:T(4,128)S(1)}, s32[256,4]{0,1:T(4,128)}, u32[]{:S(2)}) copy-start(s32[256,4]{0,1:T(4,128)} %param.26) | copy-start | bytes 12292
  56.5 6.0 %copy-start.20 = (s32[4]{0:T(128)S(1)}, s32[4]{0:T(128)}, u32[]{:S(2)}) copy-start(s32[4]{0:T(128)} %param.29) | copy-start | bytes 52
  61.7 8.0 %copy-start.6 = (bf16[256,2,128]{2,0,1:T(8,128)(2,1)}, bf16[256,2,128]{2,0,1:T(8,128)(2,1)S(1)}, u32[]{:S(2)}) copy-start(bf16[256,2,128]{2,0,1:T(8,128)(2,1)S(1)} %pad_maximum_fusion.2) | copy-start | bytes 393220
  62.6 4.4 %copy-start.9 = (f32[256,64]{0,1:T(8,128)S(1)}, f32[256,64]{0,1:T(8,128)}, u32[]{:S(2)}) copy-start(f32[256,64]{0,1:T(8,128)} %copy-done.8) | copy-start | bytes 196612
  62.6 4.5 %copy-start.11 = (f32[256,64]{0,1:T(8,128)S(1)}, f32[256,64]{0,1:T(8,128)}, u32[]{:S(2)}) copy-start(f32[256,64]{0,1:T(8,128)} %copy-done.10) | copy-start | bytes 196612
  67.3 2.5 copy-start.13
  73.1 3.1 %copy-start.15 = (bf16[4,64,2,128]{3,2,1,0:T(2,128)(2,1)S(1)}, bf16[4,64,2,128]{3,2,1,0:T(2,128)(2,1)}, u32[]{:S(2)}) copy-start(bf16[4,64,2,128]{3,2,1,0:T(2,128)(2,1)} %reshape.304) | copy-start | bytes 393220
  76.3 1.6 copy-start.5
  81.8 2.5 copy-start.3
  82.6 5.8 %copy-start.18 = (f32[1536]{0:T(1024)S(1)}, f32[1536]{0:T(1024)}, u32[]{:S(2)}) copy-start(f32[1536]{0:T(1024)} %param.22) | copy-start | bytes 18436
  90.7 40.5 %all-to-all-start = ((bf16[16,2,24,1536]{3,2,1,0:T(8,128)(2,1)}), bf16[16,2,24,1536]{3,2,1,0:T(8,128)(2,1)}, u32[]{:S(2)}, u32[]{:S(2)}) async-start(bf16[16,2,24,1536]{3,2,1,0:T(8,128)(2,1)} %bitcast.14), calls=%async_computation | async-start | bytes 4718592 | tf_op jit(solution)/shard_map/all_to_all | solution.py:157
  102.4 0.9 copy-start
  131.2 37.6 %all-to-all-start.2 = ((bf16[16,2,24,1536]{3,2,1,0:T(8,128)(2,1)}), bf16[16,2,24,1536]{3,2,1,0:T(8,128)(2,1)S(1)}, u32[]{:S(2)}, u32[]{:S(2)}) async-start(bf16[16,2,24,1536]{3,2,1,0:T(8,128)(2,1)} %bitcast.24), calls=%async_computation.2 | async-start | bytes 4718592 | tf_op jit(solution)/shard_map/all_to_all | solution.py:157
  156.9 17.4 %copy-start.7 = (bf16[256,2,128]{2,0,1:T(8,128)(2,1)S(1)}, bf16[256,2,128]{2,0,1:T(8,128)(2,1)}, u32[]{:S(2)}) copy-start(bf16[256,2,128]{2,0,1:T(8,128)(2,1)} %copy-done.6) | copy-start | bytes 393220
  156.9 17.7 %copy-start.23 = (s32[4]{0:T(128)S(1)}, s32[4]{0:T(128)}, u32[]{:S(2)}) copy-start(s32[4]{0:T(128)} %param.31) | copy-start | bytes 52
  168.9 1.4 copy-start.4
  170.3 34.3 %all-to-all-start.1 = ((bf16[16,2,24,1536]{3,2,1,0:T(8,128)(2,1)}), bf16[16,2,24,1536]{3,2,1,0:T(8,128)(2,1)S(1)}, u32[]{:S(2)}, u32[]{:S(2)}) async-start(bf16[16,2,24,1536]{3,2,1,0:T(8,128)(2,1)} %copy.136), calls=%async_computation.1 | async-start | bytes 4718592 | tf_op jit(solution)/shard_map/all_to_all | solution.py:162
  196.4 12.9 %copy-start.19 = (f32[256,4]{0,1:T(4,128)S(1)}, f32[256,4]{0,1:T(4,128)}, u32[]{:S(2)}) copy-start(f32[256,4]{0,1:T(4,128)} %param.27) | copy-start | bytes 12292
  196.4 13.3 %copy-start.14 = (bf16[256,256]{1,0:T(8,128)(2,1)S(1)}, bf16[256,256]{1,0:T(8,128)(2,1)}, u32[]{:S(2)}) copy-start(bf16[256,256]{1,0:T(8,128)(2,1)} %convolution_convert_fusion.1) | copy-start | bytes 393220
  204.6 35.2 %all-to-all-start.3 = ((bf16[16,2,24,1536]{3,2,1,0:T(8,128)(2,1)}), bf16[16,2,24,1536]{3,2,1,0:T(8,128)(2,1)}, u32[]{:S(2)}, u32[]{:S(2)}) async-start(bf16[16,2,24,1536]{3,2,1,0:T(8,128)(2,1)} %copy.140), calls=%async_computation.3 | async-start | bytes 4718592 | tf_op jit(solution)/shard_map/all_to_all | solution.py:162
  211.7 30.6 %copy-start.1 = (f32[128,1536]{1,0:T(8,128)S(1)}, f32[128,1536]{1,0:T(8,128)}, u32[]{:S(2)}) copy-start(f32[128,1536]{1,0:T(8,128)} %copy-done) | copy-start | bytes 2359300
Sparse Core Ops, SparseCore 0:
  9.7 38.5 all-gather.2
  50.0 34.2 all-gather.4
where the time goes:
time: 251 us; the launch traced here: 250 us
  waiting for transfers between devices  77 us (31%)
  matrix products  67 us (27%)
  blocking collectives  30.9 us (12%)
  local copies, waits for them, and re-layouts  30.2 us (12%)
  starting transfers between devices  21 us (8%)
  between operations  14.6 us (6%)
  other arithmetic  9.53 us (4%)
    all_to_all x2, waiting for transfers between devices, routed_whole(): lax.all_to_all(reshaped_rows, 'exp', split_axis=0, concat_axis=0, tiled=T...  37.7 us
    all_to_all x2, waiting for transfers between devices, routed_whole(): lax.all_to_all(produced, 'exp', split_axis=0, concat_axis=0, tiled=True)  36.3 us
    dot_general x2, matrix products, expert_products(): jnp.einsum('pekf,efd->pekd', hidden, w_down, preferred_element_type=jnp.f...  20.8 us
    all_gather x1, blocking collectives, local(): lax.all_gather(key_projection, 'req', axis=0, tiled=True)  15.6 us
    all_gather x1, blocking collectives, local(): lax.all_gather(value_projection, 'req', axis=0, tiled=True)  15.3 us
    dot_general x2, matrix products, expert_products(): jnp.einsum('pekd,edf->pekf', received, w_up, preferred_element_type=jnp.f...  13 us
    all_to_all x2, starting transfers between devices, routed_whole(): lax.all_to_all(reshaped_rows, 'exp', split_axis=0, concat_axis=0, tiled=T...  12.2 us
    unnamed x53, local copies, waits for them, and re-layouts  10.8 us
  transfers between devices with their start and end apart: 6, of which 5 were waited for; matrix products, arithmetic and copies ran while one was open for 37% of the time, Pallas kernels for 0%

commit v1 on v0

--- a/solution.py
+++ b/solution.py
@@ -14,6 +14,28 @@
 BLOCK_ROWS = 128
 eps_norm = 1e-06
 rope_base = 1000000.0
+
+
+def laid_out(blocks, dim):
+    lengths = list(blocks.shape[1:])
+    lengths[dim] *= blocks.shape[0]
+    return jnp.moveaxis(blocks, 0, dim).reshape(lengths)
+
+
+def ring_gather(x, axis, dim):
+    devices = lax.axis_size(axis)
+    pairs = [(i, (i + 1) % devices) for i in range(devices)]
+    back = [(b, a) for a, b in pairs]
+    lower, upper = ([], [])
+    for lap in range(devices - 1):
+        if lap % 2 == 0:
+            lower.append(lax.ppermute(lower[-1] if lower else x, axis, pairs))
+        else:
+            upper.append(lax.ppermute(upper[-1] if upper else x, axis, back))
+    blocks = jnp.stack([*lower[::-1], x, *upper])
+    shift = lax.axis_index(axis) - len(lower)
+    blocks = blocks[(jnp.arange(devices) - shift) % devices]
+    return laid_out(blocks, dim)
 
 
 def rms_scale(token_rows, gain_vec):
@@ -197,9 +219,7 @@
         preferred_element_type=jnp.float32,
     )
     value_sum = jnp.dot(
-        normed,
-        lax.all_gather(value_projection, "req", axis=0, tiled=True),
-        preferred_element_type=jnp.float32,
+        normed, ring_gather(value_projection, "req", 0), preferred_element_type=jnp.float32
     )
     query_rows = rotate(query_sum, positions).astype(jnp.bfloat16)
     tree_key_value = jnp.concatenate([rotate(key_sum, positions), value_sum], axis=1).astype(

time: 251 us -> 260 us (1.036)
  the two profiles are of different devices: /device:TPU:0 before, /device:TPU:96 now
where the time goes in v1:
time: 260 us; the launch traced here: 259 us
  waiting for transfers between devices  87.5 us (34%)
  matrix products  65.8 us (25%)
  local copies, waits for them, and re-layouts  37.2 us (14%)
  starting transfers between devices  28.5 us (11%)
  between operations  14.7 us (6%)
  blocking collectives  14.6 us (6%)
  other arithmetic  10.5 us (4%)
    all_to_all x2, waiting for transfers between devices, routed_whole(): lax.all_to_all(reshaped_rows, 'exp', split_axis=0, concat_axis=0, tiled=T...  44.1 us
    all_to_all x2, waiting for transfers between devices, routed_whole(): lax.all_to_all(produced, 'exp', split_axis=0, concat_axis=0, tiled=True)  35.5 us
    dot_general x2, matrix products, expert_products(): jnp.einsum('pekf,efd->pekd', hidden, w_down, preferred_element_type=jnp.f...  19.4 us
    unnamed x50, local copies, waits for them, and re-layouts  16.3 us
    all_gather x1, blocking collectives, local(): lax.all_gather(key_projection, 'req', axis=0, tiled=True)  14.6 us
    all_to_all x2, starting transfers between devices, routed_whole(): lax.all_to_all(reshaped_rows, 'exp', split_axis=0, concat_axis=0, tiled=T...  14.3 us
    dot_general x2, matrix products, expert_products(): jnp.einsum('pekd,edf->pekf', received, w_up, preferred_element_type=jnp.f...  13 us
    all_to_all x2, starting transfers between devices, routed_whole(): lax.all_to_all(produced, 'exp', split_axis=0, concat_axis=0, tiled=True)  8.39 us
  transfers between devices with their start and end apart: 13, of which 8 were waited for; matrix products, arithmetic and copies ran while one was open for 39% of the time, Pallas kernels for 0%

profile of v1, /device:TPU:96, one launch (start us, length us, event | category | flops | bytes accessed | tf_op | source)
XLA Modules:
  0.0 258.9 jit_solution(5359614774526087923)
XLA Ops:
  7.2 0.7 all-gather.3.cloned.1.call-update
  8.0 1.7 collective-permute-start.4
  9.8 1.3 convolution_minimum_fusion.4
  11.8 0.7 convert_add_fusion
  13.4 14.6 %all_gather.10 = bf16[1536,256]{1,0:T(8,128)(2,1)S(1)} all-gather(bf16[192,256]{1,0:T(8,128)(2,1)S(1)} %copy-done.12), channel_id=1, replica_groups=mesh['req'=8,'exp'=16] {'req'}, dimensions={0}, use_global_device_ids=true | all-gather | bytes 884736 | tf_op jit(solution)/shard_map/all_gather | solution.py:218
  29.0 4.6 %fusion.134 = (bf16[4,1024,256]{2,1,0:T(8,128)(2,1)}, bf16[4,1024,256]{2,1,0:T(8,128)(2,1)}) fusion(bf16[4,1024,512]{2,1,0:T(8,128)(2,1)} %param.28), kind=kLoop, calls=%fused_computation.179 | loop fusion | bytes 8388608 | tf_op jit(solution)/shard_map/vmap()/slice | solution.py:81
  33.9 0.8 subtract_convert_fusion.2
  34.8 0.7 copy.122
  35.5 3.0 %copy.161 = bf16[4,1024,256]{1,2,0:T(8,128)(2,1)S(1)} copy(bf16[4,1024,256]{2,1,0:T(8,128)(2,1)} %get-tuple-element.5) | data formatting | bytes 4194304
  38.5 4.0 %copy.164 = bf16[4,1024,256]{1,2,0:T(8,128)(2,1)} copy(bf16[4,1024,256]{2,1,0:T(8,128)(2,1)} %get-tuple-element.4) | data formatting | bytes 4194304
  42.5 0.4 fusion.39
  43.0 0.6 collective-permute-start.1
  43.5 1.1 pad_maximum_fusion.2
  44.6 2.6 %collective-permute-done.1 = bf16[192,256]{1,0:T(8,128)(2,1)S(1)} collective-permute-done((bf16[192,256]{1,0:T(8,128)(2,1)}, bf16[192,256]{1,0:T(8,128)(2,1)S(1)}, u32[]{:S(2)}, u32[]{:S(2)}) %collective-permute-start.1) | collective-permute-done | bytes 98336 | tf_op jit(solution)/shard_map/ppermute | solution.py:32
  47.3 1.8 collective-permute-start.5
  49.0 2.3 collective-permute-done.2
  51.5 1.7 collective-permute-start.6
  53.3 2.0 collective-permute-done.3
  55.3 0.6 bitcast_dynamic-update-slice_fusion.7
  56.0 0.6 bitcast_dynamic-update-slice_fusion.6
  56.6 0.6 bitcast_dynamic-update-slice_fusion.5
  57.3 1.5 bitcast_dynamic-update-slice_fusion.4
  58.8 1.5 bitcast_dynamic-update-slice_fusion.3
  60.3 1.5 bitcast_dynamic-update-slice_fusion.2
  61.9 0.6 bitcast_dynamic-update-slice_fusion.1
  62.5 0.6 bitcast_dynamic-update-slice_fusion
  63.2 2.6 %gather_fusion = bf16[8,192,256]{2,1,0:T(8,128)(2,1)} fusion(bf16[8,192,256]{2,1,0:T(8,128)(2,1)} %bitcast_dynamic-update-slice_fusion, s32[1024]{0:T(1024)S(1)} %pad_clamp_fusion), kind=kCustom, calls=%fused_computation | custom fusion | bytes 1572896 | tf_op jit(solution)/shard_map/gather | solution.py:37
  65.8 2.2 convolution_convert_fusion.1
  68.0 1.6 reshape.356
  69.6 4.4 %fusion.140 = f32[256,1536]{0,1:T(8,128)S(1)} fusion(bf16[256,1536]{1,0:T(8,128)(2,1)S(1)} %fusion.38, bf16[1536,1536]{1,0:T(8,128)(2,1)} %all-gather.3.cloned.1.call-done), kind=kOutput, calls=%fused_computation.185 | convolution fusion | flops 1207959552 | bytes 7077888 | tf_op jit(solution)/shard_map/dot_general | solution.py:211
  74.2 0.9 pad_maximum_fusion
  75.1 1.5 copy.118
  76.7 0.9 fusion.139
  77.6 2.1 bitcast_reduce_fusion
  80.0 3.1 %fusion.1 = f32[4,2,6,64]{3,2,1,0:T(8,128)S(1)} fusion(f32[4,2,64,6,1024]{4,2,3,1,0:T(8,128)S(1)} %get-tuple-element.25, f32[4,2,6,64]{3,2,1,0:T(8,128)S(1)} %max.25, pred[4,1024]{1,0:T(4,128)(4,1)S(1)} %iota_compare_fusion.8), kind=kLoop, calls=%fused_computation.7 | loop fusion | flops 12579840 | bytes 12611584 | tf_op jit(solution)/shard_map/vmap()/reduce_sum | solution.py:106
  83.2 0.5 fusion.74
  83.7 1.1 copy-done.4
  84.8 4.1 %fusion.40 = bf16[4,64,2,6,128]{4,1,3,2,0:T(8,128)(2,1)S(1)} fusion(f32[4,2,128,6,64]{2,4,3,1,0:T(8,128)S(1)} %fusion.74, bf16[4,1024,2,128,1]{1,3,4,2,0:T(8,128)(2,1)S(1)} %bitcast.146, f32[4,2,64,6,1024]{4,2,3,1,0:T(8,128)S(1)} %get-tuple-element.25, f32[4,2,6,64]{3,2,1,0:T(8,128)S(1)} %add.137, f32[4,2,6,64]{3,2,1,0:T(8,128)S(1)} %max.25, ...), kind=kOutput, calls=%fused_computation.47 | convolution fusion | flops 821821440 | bytes 17068032 | tf_op jit(solution)/shard_map/vmap(gsij,jgd->igsd)/dot_general | solution.py:111
  89.3 0.4 slice.81
  90.0 4.1 %multiply_reduce_fusion.1 = (f32[128]{0:T(128)S(1)}, f32[128,1536]{1,0:T(8,128)S(1)}) fusion(bf16[128,1536]{1,0:T(8,128)(2,1)S(1)} %slice.81, bf16[1536,1536]{0,1:T(8,128)(2,1)} %all-gather.5.cloned.1.call-done, bf16[256,1536]{1,0:T(8,128)(2,1)S(1)} %copy-done.1), kind=kOutput, calls=%fused_computation.76 | convolution fusion | flops 605159296 | bytes 6291968 | tf_op jit(solution)/shard_map/dot_general | solution.py:239
  94.1 2.2 fusion.78
  96.4 7.1 %all-to-all-start = ((bf16[16,2,24,1536]{3,2,1,0:T(8,128)(2,1)}), bf16[16,2,24,1536]{3,2,1,0:T(8,128)(2,1)}, u32[]{:S(2)}, u32[]{:S(2)}) async-start(bf16[16,2,24,1536]{3,2,1,0:T(8,128)(2,1)} %bitcast.26), calls=%async_computation | async-start | bytes 4718592 | tf_op jit(solution)/shard_map/all_to_all | solution.py:179
  103.8 0.4 slice.89
  104.2 4.1 %multiply_reduce_fusion = (f32[128]{0:T(128)S(1)}, f32[128,1536]{1,0:T(8,128)S(1)}) fusion(bf16[128,1536]{1,0:T(8,128)(2,1)S(1)} %slice.89, bf16[1536,1536]{0,1:T(8,128)(2,1)} %all-gather.5.cloned.1.call-done, bf16[256,1536]{1,0:T(8,128)(2,1)S(1)} %copy-done.1), kind=kOutput, calls=%fused_computation.74 | convolution fusion | flops 605159296 | bytes 6291968 | tf_op jit(solution)/shard_map/dot_general | solution.py:239
  108.3 2.3 fusion.79
  110.6 27.4 %all-to-all-done = bf16[16,2,24,1536]{3,2,1,0:T(8,128)(2,1)} async-done(((bf16[16,2,24,1536]{3,2,1,0:T(8,128)(2,1)}), bf16[16,2,24,1536]{3,2,1,0:T(8,128)(2,1)}, u32[]{:S(2)}, u32[]{:S(2)}) %all-to-all-start) | async-done | bytes 2359328 | tf_op jit(solution)/shard_map/all_to_all | solution.py:179
  138.0 7.1 %all-to-all-start.2 = ((bf16[16,2,24,1536]{3,2,1,0:T(8,128)(2,1)}), bf16[16,2,24,1536]{3,2,1,0:T(8,128)(2,1)}, u32[]{:S(2)}, u32[]{:S(2)}) async-start(bf16[16,2,24,1536]{3,2,1,0:T(8,128)(2,1)} %bitcast.36), calls=%async_computation.2 | async-start | bytes 4718592 | tf_op jit(solution)/shard_map/all_to_all | solution.py:179
  145.2 6.5 %fusion.9 = f32[2,16,24,768]{3,2,1,0:T(8,128)} fusion(bf16[2,1536,768]{2,1,0:T(8,128)(2,1)} %param.24, bf16[16,2,24,1536]{3,2,1,0:T(8,128)(2,1)} %all-to-all-done), kind=kOutput, calls=%fused_computation.15 | convolution fusion | flops 1811939328 | bytes 9437184 | tf_op jit(solution)/shard_map/pekd,edf->pekf/dot_general | solution.py:157
  151.6 9.0 %fusion.25 = bf16[16,2,24,1536]{3,2,0,1:T(8,128)(2,1)S(1)} fusion(bf16[2,768,1536]{2,1,0:T(8,128)(2,1)} %param.25, f32[2,16,24,768]{3,2,1,0:T(8,128)} %fusion.9, bf16[2,1536,768]{2,1,0:T(8,128)(2,1)} %param.23, bf16[16,2,24,1536]{3,2,1,0:T(8,128)(2,1)} %all-to-all-done), kind=kOutput, calls=%fused_computation.27 | convolution fusion | flops 3626827776 | bytes 16515072 | tf_op jit(solution)/shard_map/pekf,efd->pekd/dot_general | solution.py:159
  160.6 1.7 copy.136
  162.3 16.8 %all-to-all-done.2 = bf16[16,2,24,1536]{3,2,1,0:T(8,128)(2,1)} async-done(((bf16[16,2,24,1536]{3,2,1,0:T(8,128)(2,1)}), bf16[16,2,24,1536]{3,2,1,0:T(8,128)(2,1)}, u32[]{:S(2)}, u32[]{:S(2)}) %all-to-all-start.2) | async-done | bytes 2359328 | tf_op jit(solution)/shard_map/all_to_all | solution.py:179
  179.0 3.9 %all-to-all-start.1 = ((bf16[16,2,24,1536]{3,2,1,0:T(8,128)(2,1)}), bf16[16,2,24,1536]{3,2,1,0:T(8,128)(2,1)S(1)}, u32[]{:S(2)}, u32[]{:S(2)}) async-start(bf16[16,2,24,1536]{3,2,1,0:T(8,128)(2,1)} %copy.136), calls=%async_computation.1 | async-start | bytes 4718592 | tf_op jit(solution)/shard_map/all_to_all | solution.py:184
  183.2 0.7 concatenate.29
  183.9 1.5 gather_fusion.1
  185.4 6.5 %fusion.7 = f32[2,16,24,768]{3,2,1,0:T(8,128)} fusion(bf16[2,1536,768]{2,1,0:T(8,128)(2,1)} %param.24, bf16[16,2,24,1536]{3,2,1,0:T(8,128)(2,1)} %all-to-all-done.2), kind=kOutput, calls=%fused_computation.13 | convolution fusion | flops 1811939328 | bytes 9437184 | tf_op jit(solution)/shard_map/pekd,edf->pekf/dot_general | solution.py:157
  191.9 10.4 %fusion.22 = bf16[16,2,24,1536]{3,2,0,1:T(8,128)(2,1)} fusion(bf16[2,768,1536]{2,1,0:T(8,128)(2,1)} %param.25, f32[2,16,24,768]{3,2,1,0:T(8,128)} %fusion.7, bf16[2,1536,768]{2,1,0:T(8,128)(2,1)} %param.23, bf16[16,2,24,1536]{3,2,1,0:T(8,128)(2,1)} %all-to-all-done.2), kind=kOutput, calls=%fused_computation.26 | convolution fusion | flops 3626827776 | bytes 16515072 | tf_op jit(solution)/shard_map/pekf,efd->pekd/dot_general | solution.py:159
  202.3 3.4 %copy.140 = bf16[16,2,24,1536]{3,2,1,0:T(8,128)(2,1)} copy(bf16[16,2,24,1536]{3,2,0,1:T(8,128)(2,1)} %fusion.22) | data formatting | bytes 4718592 | tf_op jit(solution)/shard_map/convert_element_type | solution.py:159
  205.7 7.8 %all-to-all-done.1 = bf16[16,2,24,1536]{3,2,1,0:T(8,128)(2,1)S(1)} async-done(((bf16[16,2,24,1536]{3,2,1,0:T(8,128)(2,1)}), bf16[16,2,24,1536]{3,2,1,0:T(8,128)(2,1)S(1)}, u32[]{:S(2)}, u32[]{:S(2)}) %all-to-all-start.1) | async-done | bytes 2359328 | tf_op jit(solution)/shard_map/all_to_all | solution.py:184
  213.6 4.4 %all-to-all-start.3 = ((bf16[16,2,24,1536]{3,2,1,0:T(8,128)(2,1)}), bf16[16,2,24,1536]{3,2,1,0:T(8,128)(2,1)}, u32[]{:S(2)}, u32[]{:S(2)}) async-start(bf16[16,2,24,1536]{3,2,1,0:T(8,128)(2,1)} %copy.140), calls=%async_computation.3 | async-start | bytes 4718592 | tf_op jit(solution)/shard_map/all_to_all | solution.py:184
  219.0 0.9 convolution_convert_fusion
  219.9 0.8 fusion.80
  220.8 27.7 %all-to-all-done.3 = bf16[16,2,24,1536]{3,2,1,0:T(8,128)(2,1)} async-done(((bf16[16,2,24,1536]{3,2,1,0:T(8,128)(2,1)}), bf16[16,2,24,1536]{3,2,1,0:T(8,128)(2,1)}, u32[]{:S(2)}, u32[]{:S(2)}) %all-to-all-start.3) | async-done | bytes 2359328 | tf_op jit(solution)/shard_map/all_to_all | solution.py:184
  248.5 2.4 fusion.84
  251.1 0.9 pad_maximum_fusion.1
  (94 shorter events, 6.3 us)
Async XLA Ops:
  7.2 6.0 %copy-start = (bf16[256,1536]{1,0:T(8,128)(2,1)S(1)}, bf16[256,1536]{1,0:T(8,128)(2,1)}, u32[]{:S(2)}) copy-start(bf16[256,1536]{1,0:T(8,128)(2,1)} %param.16) | copy-start | bytes 2359300
  7.2 6.2 %copy-start.12 = (bf16[192,256]{1,0:T(8,128)(2,1)S(1)}, bf16[192,256]{1,0:T(8,128)(2,1)}, u32[]{:S(2)}) copy-start(bf16[192,256]{1,0:T(8,128)(2,1)} %param.19) | copy-start | bytes 294916
  7.2 20.8 %copy-start.15 = (f32[1536]{0:T(1024)S(1)}, f32[1536]{0:T(1024)}, u32[]{:S(2)}) copy-start(f32[1536]{0:T(1024)} %param.17) | copy-start | bytes 18436
  7.2 62.4 %all-gather.3.cloned.1.call-start = ((), (), s32[]{:S(2)}) async-start(), calls=%async_computation.4 | async-start | bytes 5308416 | tf_op jit(solution)/shard_map/all_gather | solution.py:213
  7.9 81.8 %all-gather.5.cloned.1.call-start = ((), (), s32[]{:S(2)}) async-start(), calls=%async_computation.5 | async-start | bytes 5308416 | tf_op jit(solution)/shard_map/all_gather | solution.py:230
  8.0 35.0 %collective-permute-start = (bf16[192,256]{1,0:T(8,128)(2,1)}, bf16[192,256]{1,0:T(8,128)(2,1)}, u32[]{:S(2)}, u32[]{:S(2)}) collective-permute-start(bf16[192,256]{1,0:T(8,128)(2,1)} %param.20), channel_id=1, source_target_pairs={{0,16},{16,32},{32,48},{48,64},{64,80},{80,96},{96,112},{112,0},{1... | collective-permute-start | bytes 294920 | tf_op jit(solution)/shard_map/ppermute | solution.py:32
  8.0 39.2 %collective-permute-start.4 = (bf16[192,256]{1,0:T(8,128)(2,1)}, bf16[192,256]{1,0:T(8,128)(2,1)}, u32[]{:S(2)}, u32[]{:S(2)}) collective-permute-start(bf16[192,256]{1,0:T(8,128)(2,1)} %param.20), channel_id=1, source_target_pairs={{16,0},{32,16},{48,32},{64,48},{80,64},{96,80},{112,96},{0,112},{1... | collective-permute-start | bytes 294920 | tf_op jit(solution)/shard_map/ppermute | solution.py:34
  11.7 1.7 copy-start.8
  29.0 4.6 %copy-start.13 = (s32[256,4]{0,1:T(4,128)S(1)}, s32[256,4]{0,1:T(4,128)}, u32[]{:S(2)}) copy-start(s32[256,4]{0,1:T(4,128)} %param.26) | copy-start | bytes 12292
  29.0 5.7 %copy-start.17 = (s32[4]{0:T(128)S(1)}, s32[4]{0:T(128)}, u32[]{:S(2)}) copy-start(s32[4]{0:T(128)} %param.29) | copy-start | bytes 52
  43.0 4.3 %collective-permute-start.1 = (bf16[192,256]{1,0:T(8,128)(2,1)}, bf16[192,256]{1,0:T(8,128)(2,1)S(1)}, u32[]{:S(2)}, u32[]{:S(2)}) collective-permute-start(bf16[192,256]{1,0:T(8,128)(2,1)} %collective-permute-done), channel_id=1, source_target_pairs={{0,16},{16,32},{32,48},{48,64},{64,80},{80,96},{96,112},{112,0},{1... | collective-permute-start | bytes 294920 | tf_op jit(solution)/shard_map/ppermute | solution.py:32
  44.6 32.1 %copy-start.5 = (bf16[256,2,128]{2,0,1:T(8,128)(2,1)}, bf16[256,2,128]{2,0,1:T(8,128)(2,1)S(1)}, u32[]{:S(2)}) copy-start(bf16[256,2,128]{2,0,1:T(8,128)(2,1)S(1)} %pad_maximum_fusion.2) | copy-start | bytes 393220
  47.2 4.0 %collective-permute-start.2 = (bf16[192,256]{1,0:T(8,128)(2,1)S(1)}, bf16[192,256]{1,0:T(8,128)(2,1)S(1)}, u32[]{:S(2)}, u32[]{:S(2)}) collective-permute-start(bf16[192,256]{1,0:T(8,128)(2,1)S(1)} %collective-permute-done.1), channel_id=1, source_target_pairs={{0,16},{16,32},{32,48},{48,64},{64,80},{80,96},{96,112},{112,0},{1... | collective-permute-start | bytes 294920 | tf_op jit(solution)/shard_map/ppermute | solution.py:32
  47.3 4.3 %collective-permute-start.5 = (bf16[192,256]{1,0:T(8,128)(2,1)}, bf16[192,256]{1,0:T(8,128)(2,1)S(1)}, u32[]{:S(2)}, u32[]{:S(2)}) collective-permute-start(bf16[192,256]{1,0:T(8,128)(2,1)} %collective-permute-done.4), channel_id=1, source_target_pairs={{16,0},{32,16},{48,32},{64,48},{80,64},{96,80},{112,96},{0,112},{1... | collective-permute-start | bytes 294920 | tf_op jit(solution)/shard_map/ppermute | solution.py:34
  51.3 4.0 %collective-permute-start.3 = (bf16[192,256]{1,0:T(8,128)(2,1)S(1)}, bf16[192,256]{1,0:T(8,128)(2,1)S(1)}, u32[]{:S(2)}, u32[]{:S(2)}) collective-permute-start(bf16[192,256]{1,0:T(8,128)(2,1)S(1)} %collective-permute-done.2), channel_id=1, source_target_pairs={{0,16},{16,32},{32,48},{48,64},{64,80},{80,96},{96,112},{112,0},{1... | collective-permute-start | bytes 294920 | tf_op jit(solution)/shard_map/ppermute | solution.py:32
  51.5 11.0 %collective-permute-start.6 = (bf16[192,256]{1,0:T(8,128)(2,1)S(1)}, bf16[192,256]{1,0:T(8,128)(2,1)S(1)}, u32[]{:S(2)}, u32[]{:S(2)}) collective-permute-start(bf16[192,256]{1,0:T(8,128)(2,1)S(1)} %collective-permute-done.5), channel_id=1, source_target_pairs={{16,0},{32,16},{48,32},{64,48},{80,64},{96,80},{112,96},{0,112},{1... | collective-permute-start | bytes 294920 | tf_op jit(solution)/shard_map/ppermute | solution.py:34
  74.2 2.5 copy-start.9
  80.0 3.1 %copy-start.11 = (bf16[4,64,2,128]{3,2,1,0:T(2,128)(2,1)S(1)}, bf16[4,64,2,128]{3,2,1,0:T(2,128)(2,1)}, u32[]{:S(2)}) copy-start(bf16[4,64,2,128]{3,2,1,0:T(2,128)(2,1)} %reshape.356) | copy-start | bytes 393220
  83.2 1.6 copy-start.4
  88.9 1.1 copy-start.1
  89.7 4.4 %copy-start.14 = (f32[1536]{0:T(1024)S(1)}, f32[1536]{0:T(1024)}, u32[]{:S(2)}) copy-start(f32[1536]{0:T(1024)} %param.22) | copy-start | bytes 18436
  96.4 41.6 %all-to-all-start = ((bf16[16,2,24,1536]{3,2,1,0:T(8,128)(2,1)}), bf16[16,2,24,1536]{3,2,1,0:T(8,128)(2,1)}, u32[]{:S(2)}, u32[]{:S(2)}) async-start(bf16[16,2,24,1536]{3,2,1,0:T(8,128)(2,1)} %bitcast.26), calls=%async_computation | async-start | bytes 4718592 | tf_op jit(solution)/shard_map/all_to_all | solution.py:179
  108.3 29.7 %copy-start.2 = (f32[128,1536]{1,0:T(8,128)}, f32[128,1536]{1,0:T(8,128)S(1)}, u32[]{:S(2)}) copy-start(f32[128,1536]{1,0:T(8,128)S(1)} %get-tuple-element.29) | copy-start | bytes 2359300
  138.0 41.0 %all-to-all-start.2 = ((bf16[16,2,24,1536]{3,2,1,0:T(8,128)(2,1)}), bf16[16,2,24,1536]{3,2,1,0:T(8,128)(2,1)}, u32[]{:S(2)}, u32[]{:S(2)}) async-start(bf16[16,2,24,1536]{3,2,1,0:T(8,128)(2,1)} %bitcast.36), calls=%async_computation.2 | async-start | bytes 4718592 | tf_op jit(solution)/shard_map/all_to_all | solution.py:179
  162.3 20.7 %copy-start.6 = (bf16[256,2,128]{2,0,1:T(8,128)(2,1)S(1)}, bf16[256,2,128]{2,0,1:T(8,128)(2,1)}, u32[]{:S(2)}) copy-start(bf16[256,2,128]{2,0,1:T(8,128)(2,1)} %copy-done.5) | copy-start | bytes 393220
  162.3 21.6 %copy-start.18 = (s32[4]{0:T(128)S(1)}, s32[4]{0:T(128)}, u32[]{:S(2)}) copy-start(s32[4]{0:T(128)} %param.31) | copy-start | bytes 52
  179.0 34.5 %all-to-all-start.1 = ((bf16[16,2,24,1536]{3,2,1,0:T(8,128)(2,1)}), bf16[16,2,24,1536]{3,2,1,0:T(8,128)(2,1)S(1)}, u32[]{:S(2)}, u32[]{:S(2)}) async-start(bf16[16,2,24,1536]{3,2,1,0:T(8,128)(2,1)} %copy.136), calls=%async_computation.1 | async-start | bytes 4718592 | tf_op jit(solution)/shard_map/all_to_all | solution.py:184
  205.7 12.3 %copy-start.16 = (f32[256,4]{0,1:T(4,128)S(1)}, f32[256,4]{0,1:T(4,128)}, u32[]{:S(2)}) copy-start(f32[256,4]{0,1:T(4,128)} %param.27) | copy-start | bytes 12292
  213.6 34.9 %all-to-all-start.3 = ((bf16[16,2,24,1536]{3,2,1,0:T(8,128)(2,1)}), bf16[16,2,24,1536]{3,2,1,0:T(8,128)(2,1)}, u32[]{:S(2)}, u32[]{:S(2)}) async-start(bf16[16,2,24,1536]{3,2,1,0:T(8,128)(2,1)} %copy.140), calls=%async_computation.3 | async-start | bytes 4718592 | tf_op jit(solution)/shard_map/all_to_all | solution.py:184
  218.0 0.9 copy-start.7
  218.0 1.0 copy-start.10
  220.8 30.1 %copy-start.3 = (f32[128,1536]{1,0:T(8,128)S(1)}, f32[128,1536]{1,0:T(8,128)}, u32[]{:S(2)}) copy-start(f32[128,1536]{1,0:T(8,128)} %copy-done.2) | copy-start | bytes 2359300
Sparse Core Ops, SparseCore 0:
  9.7 34.0 all-gather.2
  45.5 34.9 all-gather.4
